TPU v7x, 32 devices: a whole 2x2x4 slice. The times are simulated.
32 devices in a mesh: pp: 2 (over y), ep: 16 (over z, x, core).
Axes of the slice: x: 2, y: 2, z: 4, core: 2. Of those that a mesh axis runs over, the one named last changes fastest.
Arguments:
- fwd_input: bfloat16 [2, 512, 7168], P('pp', 'ep'), may hold values from -6 to 6
- fwd_experts: int32 [2, 512, 2], P('pp', 'ep'), may hold values from 0 to 3, all different within a row; in each aligned block of 32 rows (0 to 31, 32 to 63, ..., all dimensions but the last counted through in order) at most 24 rows name the same one
- fwd_gates: float32 [2, 512, 2], P('pp', 'ep'), may hold values from 0.1 to 1
- bwd_input: bfloat16 [2, 512, 7168], P('pp', 'ep'), may hold values from -6 to 6
- bwd_grad: bfloat16 [2, 512, 7168], P('pp', 'ep'), may hold values from -6 to 6
- bwd_experts: int32 [2, 512, 2], P('pp', 'ep'), may hold values from 0 to 3, all different within a row; in each aligned block of 32 rows (0 to 31, 32 to 63, ..., all dimensions but the last counted through in order) at most 24 rows name the same one
- bwd_gates: float32 [2, 512, 2], P('pp', 'ep'), may hold values from 0.1 to 1
- gate_proj: bfloat16 [2, 7168, 4096], P('pp', None, 'ep'), may hold values from -0.0625 to 0.0625
- up_proj: bfloat16 [2, 7168, 4096], P('pp', None, 'ep'), may hold values from -0.0625 to 0.0625
- down_proj: bfloat16 [2, 4096, 7168], P('pp', 'ep'), may hold values from -0.1875 to 0.1875
Outputs:
- next_section_input: bfloat16 [2, 512, 7168], P('pp', 'ep')
- prev_section_grad: bfloat16 [2, 512, 7168], P('pp', 'ep')
Inputs may be any that keep to these rules, and one draw needn't show every extreme that they name: `fwd_experts`: each token names 2 different experts; in each device's aligned block of 32 tokens no expert is named more than 24 times, a bound that some block reaches. `bwd_experts`: each token names 2 different experts; in each device's aligned block of 32 tokens no expert is named more than 24 times, a bound that some block reaches.
All inputs are finite; a program needn't handle non-finite values.
Results may differ from a plain program's by a relative error of at most 0.0075.
Values may be sent and summed in bfloat16 or wider, within the bound.
No kernel may reach another device: no remote copies, remote signals or barrier semaphores. Data moves between devices by JAX's collectives and lax.ppermute only.
A program may use at most 128 MiB of HBM per device.

v0:
```python
import jax
import jax.numpy as jnp
from jax import lax
from jax.sharding import PartitionSpec as P

GROUP = 4
TOPK = 2


def from_partner(block, axis, apart):
    count = lax.axis_size(axis)
    route = []
    for low in range(count):
        high = low | 1 << apart
        if high != low and high < count:
            route += [(low, high), (high, low)]
    return lax.ppermute(block, axis, route)


def passed_along(value, axis, steps):
    count = lax.axis_size(axis)
    pairs = [(source, (source + steps) % count) for source in range(count)]
    return lax.ppermute(value, axis, pairs)


def routing(ids, gates, experts, capacity):
    pairs = ids.reshape(-1)
    hot = (pairs[:, None] == jnp.arange(experts, dtype=jnp.int32)[None, :]).astype(jnp.int32)
    before = jnp.cumsum(hot, axis=0) - hot
    slot = jnp.sum(hot * before, axis=1)
    target = (pairs * capacity + slot).reshape(ids.shape)
    columns = jnp.arange(experts * capacity, dtype=jnp.int32)
    match = (target[:, :, None] == columns[None, None, :]).astype(jnp.float32)
    select = jnp.sum(match, axis=1).astype(jnp.bfloat16)
    weights = jnp.sum(gates[:, :, None] * match, axis=1)
    return (select, weights)


def into_slots(select, rows_in):
    placed = lax.dot_general(
        select, rows_in, (((0,), (0,)), ((), ())), preferred_element_type=jnp.float32
    )
    return placed.astype(jnp.bfloat16)


def make_forward(w_gate, w_up, w_down):

    def forward_rows(received):
        lead, count, width = received.shape
        rows_in = received.reshape(lead * count, width)
        g = jnp.dot(rows_in, w_gate, preferred_element_type=jnp.float32)
        u = jnp.dot(rows_in, w_up, preferred_element_type=jnp.float32)
        hidden = (g * jax.nn.sigmoid(g) * u).astype(jnp.bfloat16)
        part = jnp.dot(hidden, w_down, preferred_element_type=jnp.float32).astype(jnp.bfloat16)
        return part.reshape(lead, count, w_down.shape[1])

    return forward_rows


def make_backward(w_gate, w_up, w_down):
    width = w_gate.shape[0]

    def backward_rows(received):
        lead, count, _ = received.shape
        rows_all = received.reshape(lead * count, 2 * width)
        rows_in = rows_all[:, :width]
        rows_grad = rows_all[:, width:]
        g = jnp.dot(rows_in, w_gate, preferred_element_type=jnp.float32)
        u = jnp.dot(rows_in, w_up, preferred_element_type=jnp.float32)
        dh = lax.dot_general(
            rows_grad, w_down, (((1,), (1,)), ((), ())), preferred_element_type=jnp.float32
        )
        sig = jax.nn.sigmoid(g)
        grad_gate = (dh * u * sig * (1.0 + g * (1.0 - sig))).astype(jnp.bfloat16)
        grad_up = (dh * g * sig).astype(jnp.bfloat16)
        part = lax.dot_general(
            grad_gate, w_gate, (((1,), (1,)), ((), ())), preferred_element_type=jnp.float32
        )
        part = part + lax.dot_general(
            grad_up, w_up, (((1,), (1,)), ((), ())), preferred_element_type=jnp.float32
        )
        return part.astype(jnp.bfloat16).reshape(lead, count, width)

    return backward_rows


def fill_group(shares, backward):
    index = lax.axis_index("ep")
    gathered = shares[:, None]
    for bit in range(GROUP.bit_length() - 1):
        if backward:
            other = from_partner(gathered, "ep", bit)
        else:
            other = from_partner(gathered, "ep", bit)
        upper = index >> bit & 1 == 1
        gathered = jnp.where(
            upper,
            jnp.concatenate([other, gathered], axis=1),
            jnp.concatenate([gathered, other], axis=1),
        )
    lead = gathered.shape[0]
    return gathered.reshape(lead, -1, gathered.shape[3])


def body(
    fwd_input,
    fwd_experts,
    fwd_gates,
    bwd_input,
    bwd_grad,
    bwd_experts,
    bwd_gates,
    gate_proj,
    up_proj,
    down_proj,
):
    devices = lax.axis_size("ep")
    experts = devices // GROUP
    tokens = fwd_input.shape[1]
    width = fwd_input.shape[2]
    capacity = min(tokens, 3 * tokens * TOPK // (2 * experts))
    w_gate = gate_proj[0]
    w_up = up_proj[0]
    w_down = down_proj[0]
    forward_rows = make_forward(w_gate, w_up, w_down)
    backward_rows = make_backward(w_gate, w_up, w_down)
    f_select, f_weights = routing(fwd_experts[0], fwd_gates[0], experts, capacity)
    b_select, b_weights = routing(bwd_experts[0], bwd_gates[0], experts, capacity)
    f_slots = into_slots(f_select, fwd_input[0]).reshape(experts, capacity, width)
    b_joined = jnp.concatenate([bwd_input[0], bwd_grad[0]], axis=1)
    b_slots = into_slots(b_select, b_joined).reshape(experts, capacity, 2 * width)
    f_shares = lax.all_to_all(
        f_slots.reshape(devices, capacity // GROUP, width),
        "ep",
        split_axis=0,
        concat_axis=0,
        tiled=True,
    )
    f_partial = forward_rows(fill_group(f_shares, False))
    b_shares = lax.all_to_all(
        b_slots.reshape(devices, capacity // GROUP, 2 * width),
        "ep",
        split_axis=0,
        concat_axis=0,
        tiled=True,
    )
    b_partial = backward_rows(fill_group(b_shares, True))
    f_back = lax.all_to_all(f_partial, "ep", split_axis=0, concat_axis=0, tiled=True)
    f_out = jnp.sum(
        f_back.reshape(experts, GROUP, capacity, width).astype(jnp.float32), axis=1
    ).astype(jnp.bfloat16)
    b_back = lax.all_to_all(b_partial, "ep", split_axis=0, concat_axis=0, tiled=True)
    b_out = jnp.sum(
        b_back.reshape(experts, GROUP, capacity, width).astype(jnp.float32), axis=1
    ).astype(jnp.bfloat16)
    high = lax.Precision.HIGHEST
    f_mixed = jnp.dot(
        f_weights, f_out.reshape(experts * capacity, width).astype(jnp.float32), precision=high
    )
    f_result = (fwd_input[0].astype(jnp.float32) + f_mixed).astype(jnp.bfloat16)
    b_mixed = jnp.dot(
        b_weights, b_out.reshape(experts * capacity, width).astype(jnp.float32), precision=high
    )
    b_result = (bwd_grad[0].astype(jnp.float32) + b_mixed).astype(jnp.bfloat16)
    next_section_input = passed_along(f_result[None], "pp", 1)
    prev_section_grad = passed_along(b_result[None], "pp", -1)
    return (next_section_input, prev_section_grad)


def solution(mesh):
    in_specs = (
        P("pp", "ep", None),
        P("pp", "ep", None),
        P("pp", "ep", None),
        P("pp", "ep", None),
        P("pp", "ep", None),
        P("pp", "ep", None),
        P("pp", "ep", None),
        P("pp", None, "ep"),
        P("pp", None, "ep"),
        P("pp", "ep", None),
    )
    out_specs = (P("pp", "ep", None), P("pp", "ep", None))
    return jax.shard_map(body, mesh=mesh, in_specs=in_specs, out_specs=out_specs, check_vma=False)
```

profile of v0, /device:TPU:10, one launch (start us, length us, event | category | flops | bytes accessed | tf_op | source)
XLA Modules:
  0.0 562.2 jit_solution(15178722693794301228)
XLA Ops:
  3.5 1.5 convolution_convert_fusion.2
  5.1 1.5 reshape_reshape.8
  6.6 6.3 %all-to-all-start = ((bf16[16,6,7168]{2,1,0:T(8,128)(2,1)}), bf16[16,6,7168]{2,1,0:T(8,128)(2,1)S(1)}, u32[]{:S(2)}, u32[]{:S(2)}) async-start(bf16[16,6,7168]{2,1,0:T(8,128)(2,1)} %reshape_reshape.8), calls=%async_computation | async-start | bytes 3670016 | tf_op jit(solution)/shard_map/all_to_all | solution.py:132
  13.8 2.4 convolution_convert_fusion
  16.2 4.6 reshape_reshape.9
  20.8 33.7 %all-to-all-done = bf16[16,6,7168]{2,1,0:T(8,128)(2,1)S(1)} async-done(((bf16[16,6,7168]{2,1,0:T(8,128)(2,1)}), bf16[16,6,7168]{2,1,0:T(8,128)(2,1)S(1)}, u32[]{:S(2)}, u32[]{:S(2)}) %all-to-all-start) | async-done | bytes 1376288 | tf_op jit(solution)/shard_map/all_to_all | solution.py:132
  54.5 5.5 all-to-all-start.2
  60.0 1.9 copy.54
  62.0 3.2 collective-permute-done
  65.2 0.8 copy.55
  66.0 1.0 maximum_select_fusion.3
  67.0 1.8 copy-done.1
  68.8 3.1 copy.57
  72.5 68.7 %all-to-all-done.2 = bf16[16,6,14336]{2,1,0:T(8,128)(2,1)} async-done(((bf16[16,6,14336]{2,1,0:T(8,128)(2,1)}), bf16[16,6,14336]{2,1,0:T(8,128)(2,1)}, u32[]{:S(2)}, u32[]{:S(2)}) %all-to-all-start.2) | async-done | bytes 2752544 | tf_op jit(solution)/shard_map/all_to_all | solution.py:140
  141.2 5.1 copy.63
  146.8 13.3 %collective-permute-done.1 = bf16[16,2,6,7168]{3,0,2,1:T(8,128)(2,1)} collective-permute-done((bf16[16,2,6,7168]{3,0,2,1:T(8,128)(2,1)}, bf16[16,2,6,7168]{3,0,2,1:T(8,128)(2,1)}, u32[]{:S(2)}, u32[]{:S(2)}) %collective-permute-start.1) | collective-permute-done | bytes 2752544 | tf_op jit(solution)/shard_map/ppermute | solution.py:17
  160.1 3.3 copy.58
  163.4 3.2 maximum_select_fusion.1
  166.6 3.6 copy.60
  170.2 8.6 %select_n.54 = bf16[384,7168]{1,0:T(8,128)(2,1)} reshape(bf16[16,4,6,7168]{3,2,1,0:T(8,128)(2,1)} %copy.60) | data formatting | bytes 11010048 | tf_op jit(solution)/shard_map/jit(_where)/select_n | solution.py:96
  178.8 5.3 fusion.19
  184.0 1.5 copy.64
  185.6 6.2 %maximum_select_fusion.2 = bf16[16,2,6,14336]{3,2,0,1:T(8,128)(2,1)S(1)} fusion(bf16[16,1,6,14336]{3,2,0,1:T(8,128)(2,1)} %bitcast.15, bf16[16,1,6,14336]{3,2,0,1:T(8,128)(2,1)S(1)} %copy.64, pred[]{:T(512)S(6)} %eq.72), kind=kLoop, calls=%fused_computation.12 | loop fusion | flops 8257536 | bytes 11010049 | tf_op jit(solution)/shard_map/jit(_where)/select_n | solution.py:96
  191.8 5.4 copy.66
  197.4 1.5 collective-permute-start.4
  198.8 1.6 fusion.44
  200.4 4.0 convolution_convert_fusion.1
  204.4 6.6 %all-to-all-start.1 = ((bf16[16,24,7168]{2,1,0:T(8,128)(2,1)}), bf16[16,24,7168]{2,1,0:T(8,128)(2,1)}, u32[]{:S(2)}, u32[]{:S(2)}) async-start(bf16[16,24,7168]{2,1,0:T(8,128)(2,1)} %bitcast.71), calls=%async_computation.1 | async-start | bytes 11010048 | tf_op jit(solution)/shard_map/all_to_all | solution.py:148
  211.0 152.5 %collective-permute-done.4 = bf16[16,2,6,14336]{3,0,2,1:T(8,128)(2,1)} collective-permute-done((bf16[16,2,6,14336]{3,0,2,1:T(8,128)(2,1)}, bf16[16,2,6,14336]{3,0,2,1:T(8,128)(2,1)}, u32[]{:S(2)}, u32[]{:S(2)}) %collective-permute-start.4) | collective-permute-done | bytes 5505056 | tf_op jit(solution)/shard_map/ppermute | solution.py:17
  363.5 5.6 %copy.67 = bf16[16,2,6,14336]{3,2,0,1:T(8,128)(2,1)S(1)} copy(bf16[16,2,6,14336]{3,0,2,1:T(8,128)(2,1)} %collective-permute-done.4) | data formatting | bytes 11010048 | tf_op jit(solution)/shard_map/ppermute | solution.py:17
  369.2 6.3 %maximum_select_fusion = bf16[16,4,6,14336]{3,2,0,1:T(8,128)(2,1)S(1)} fusion(bf16[16,2,6,14336]{3,2,0,1:T(8,128)(2,1)S(1)} %bitcast.69, bf16[16,2,6,14336]{3,2,0,1:T(8,128)(2,1)S(1)} %copy.67, pred[]{:T(512)S(6)} %eq.71), kind=kLoop, calls=%fused_computation.1 | loop fusion | flops 16515072 | bytes 22020096 | tf_op jit(solution)/shard_map/jit(_where)/select_n | solution.py:96
  375.4 6.6 %copy.69 = bf16[16,4,6,14336]{3,2,1,0:T(8,128)(2,1)} copy(bf16[16,4,6,14336]{3,2,0,1:T(8,128)(2,1)S(1)} %maximum_select_fusion) | data formatting | bytes 22020096 | tf_op jit(solution)/shard_map/jit(_where)/select_n | solution.py:96
  382.1 16.5 %select_n.59 = bf16[384,14336]{1,0:T(8,128)(2,1)} reshape(bf16[16,4,6,14336]{3,2,1,0:T(8,128)(2,1)} %copy.69) | data formatting | bytes 22020096 | tf_op jit(solution)/shard_map/jit(_where)/select_n | solution.py:96
  398.6 5.4 fusion.4
  404.0 1.4 copy-done.3
  405.4 3.8 fusion.6
  409.2 1.6 fusion.39
  411.2 1.6 fusion.16
  412.9 4.1 add_convert_fusion
  416.9 6.0 %all-to-all-start.3 = ((bf16[16,24,7168]{2,1,0:T(8,128)(2,1)}), bf16[16,24,7168]{2,1,0:T(8,128)(2,1)}, u32[]{:S(2)}, u32[]{:S(2)}) async-start(bf16[16,24,7168]{2,1,0:T(8,128)(2,1)} %bitcast.70), calls=%async_computation.3 | async-start | bytes 11010048 | tf_op jit(solution)/shard_map/all_to_all | solution.py:152
  423.0 3.6 bitcast_reduce_fusion.1
  427.3 1.6 collective-permute-start.2
  428.9 114.5 %all-to-all-done.3 = bf16[16,24,7168]{2,1,0:T(8,128)(2,1)} async-done(((bf16[16,24,7168]{2,1,0:T(8,128)(2,1)}), bf16[16,24,7168]{2,1,0:T(8,128)(2,1)}, u32[]{:S(2)}, u32[]{:S(2)}) %all-to-all-start.3) | async-done | bytes 5505056 | tf_op jit(solution)/shard_map/all_to_all | solution.py:152
  543.4 3.5 bitcast_reduce_fusion
  547.6 1.6 collective-permute-start.5
  549.2 11.2 %collective-permute-done.5 = bf16[1,32,7168]{2,1,0:T(8,128)(2,1)S(1)} collective-permute-done((bf16[1,32,7168]{2,1,0:T(8,128)(2,1)S(1)}, bf16[1,32,7168]{2,1,0:T(8,128)(2,1)S(1)}, u32[]{:S(2)}, u32[]{:S(2)}) %collective-permute-start.5) | collective-permute-done | bytes 458784 | tf_op jit(solution)/shard_map/ppermute | solution.py:23
  560.4 0.8 copy.72
  561.2 0.8 copy.73
  (62 shorter events, 7.0 us)
Async XLA Ops:
  5.1 7.8 %copy-start.12 = (s32[1,32,2]{1,2,0:T(2,128)S(1)}, s32[1,32,2]{1,2,0:T(2,128)}, u32[]{:S(2)}) copy-start(s32[1,32,2]{1,2,0:T(2,128)} %param.15) | copy-start | bytes 772
  5.1 8.6 %copy-start.13 = (f32[1,32,2]{1,2,0:T(2,128)S(1)}, f32[1,32,2]{1,2,0:T(2,128)}, u32[]{:S(2)}) copy-start(f32[1,32,2]{1,2,0:T(2,128)} %param.16) | copy-start | bytes 772
  5.1 8.7 %copy-start.9 = (bf16[1,32,7168]{2,1,0:T(8,128)(2,1)S(1)}, bf16[1,32,7168]{2,1,0:T(8,128)(2,1)}, u32[]{:S(2)}) copy-start(bf16[1,32,7168]{2,1,0:T(8,128)(2,1)} %param.14) | copy-start | bytes 1376260
  5.1 8.7 %copy-start.11 = (bf16[1,32,7168]{2,1,0:T(8,128)(2,1)S(1)}, bf16[1,32,7168]{2,1,0:T(8,128)(2,1)}, u32[]{:S(2)}) copy-start(bf16[1,32,7168]{2,1,0:T(8,128)(2,1)} %param.13) | copy-start | bytes 1376260
  6.6 47.9 %all-to-all-start = ((bf16[16,6,7168]{2,1,0:T(8,128)(2,1)}), bf16[16,6,7168]{2,1,0:T(8,128)(2,1)S(1)}, u32[]{:S(2)}, u32[]{:S(2)}) async-start(bf16[16,6,7168]{2,1,0:T(8,128)(2,1)} %reshape_reshape.8), calls=%async_computation | async-start | bytes 3670016 | tf_op jit(solution)/shard_map/all_to_all | solution.py:132
  54.5 86.6 %all-to-all-start.2 = ((bf16[16,6,14336]{2,1,0:T(8,128)(2,1)}), bf16[16,6,14336]{2,1,0:T(8,128)(2,1)}, u32[]{:S(2)}, u32[]{:S(2)}) async-start(bf16[16,6,14336]{2,1,0:T(8,128)(2,1)} %reshape_reshape.9), calls=%async_computation.2 | async-start | bytes 7340032 | tf_op jit(solution)/shard_map/all_to_all | solution.py:140
  61.9 3.3 collective-permute-start
  67.0 1.8 copy-start.1
  71.9 88.2 %collective-permute-start.1 = (bf16[16,2,6,7168]{3,0,2,1:T(8,128)(2,1)}, bf16[16,2,6,7168]{3,0,2,1:T(8,128)(2,1)}, u32[]{:S(2)}, u32[]{:S(2)}) collective-permute-start(bf16[16,2,6,7168]{3,0,2,1:T(8,128)(2,1)} %copy.57), channel_id=1, source_target_pairs={{0,2},{2,0},{1,3},{3,1},{4,6},{6,4},{5,7},{7,5},{8,10},{10,8},{9,1... | collective-permute-start | bytes 8257544 | tf_op jit(solution)/shard_map/ppermute | solution.py:17
  146.3 37.8 %collective-permute-start.3 = (bf16[16,1,6,14336]{3,0,2,1:T(8,128)(2,1)}, bf16[16,1,6,14336]{3,0,2,1:T(8,128)(2,1)S(1)}, u32[]{:S(2)}, u32[]{:S(2)}) collective-permute-start(bf16[16,1,6,14336]{3,0,2,1:T(8,128)(2,1)} %copy.63), channel_id=1, source_target_pairs={{0,1},{1,0},{2,3},{3,2},{4,5},{5,4},{6,7},{7,6},{8,9},{9,8},{10,11... | collective-permute-start | bytes 8257544 | tf_op jit(solution)/shard_map/ppermute | solution.py:17
  146.8 16.6 %copy-start.2 = (bf16[16,2,6,7168]{3,2,0,1:T(8,128)(2,1)S(1)}, bf16[16,2,6,7168]{3,2,0,1:T(8,128)(2,1)}, u32[]{:S(2)}) copy-start(bf16[16,2,6,7168]{3,2,0,1:T(8,128)(2,1)} %copy-done.1) | copy-start | bytes 8257540
  184.0 14.8 %slice-start.2 = ((s8[5505024]{0:T(1024)(128)(4,1)}), s8[4194304]{0:T(1024)(128)(4,1)S(1)}, s32[]{:S(2)}) async-start(s8[5505024]{0:T(1024)(128)(4,1)} %bitcast.74), calls=%async_computation.6 | async-start | bytes 8388608
  185.6 13.2 %slice-start.3 = ((s8[5505024]{0:T(1024)(128)(4,1)}), s8[1310720]{0:T(1024)(128)(4,1)S(1)}, s32[]{:S(2)}) async-start(s8[5505024]{0:T(1024)(128)(4,1)} %bitcast.74), calls=%async_computation.7 | async-start | bytes 2621440
  191.8 5.6 copy-start
  191.8 7.0 %copy-start.5 = (bf16[1,7168,256]{2,1,0:T(8,128)(2,1)S(1)}, bf16[1,7168,256]{2,1,0:T(8,128)(2,1)}, u32[]{:S(2)}) copy-start(bf16[1,7168,256]{2,1,0:T(8,128)(2,1)} %param.18) | copy-start | bytes 11010052
  197.4 3.1 copy-start.7
  197.4 166.1 %collective-permute-start.4 = (bf16[16,2,6,14336]{3,0,2,1:T(8,128)(2,1)}, bf16[16,2,6,14336]{3,0,2,1:T(8,128)(2,1)}, u32[]{:S(2)}, u32[]{:S(2)}) collective-permute-start(bf16[16,2,6,14336]{3,0,2,1:T(8,128)(2,1)} %copy.66), channel_id=1, source_target_pairs={{0,2},{2,0},{1,3},{3,1},{4,6},{6,4},{5,7},{7,5},{8,10},{10,8},{9,1... | collective-permute-start | bytes 16515080 | tf_op jit(solution)/shard_map/ppermute | solution.py:17
  204.4 164.7 %slice-start = ((s8[7340032]{0:T(1024)(128)(4,1)}), s8[3145728]{0:T(1024)(128)(4,1)S(1)}, s32[]{:S(2)}) async-start(s8[7340032]{0:T(1024)(128)(4,1)} %bitcast.68), calls=%async_computation.4 | async-start | bytes 6291456
  204.4 212.5 %all-to-all-start.1 = ((bf16[16,24,7168]{2,1,0:T(8,128)(2,1)}), bf16[16,24,7168]{2,1,0:T(8,128)(2,1)}, u32[]{:S(2)}, u32[]{:S(2)}) async-start(bf16[16,24,7168]{2,1,0:T(8,128)(2,1)} %bitcast.71), calls=%async_computation.1 | async-start | bytes 11010048 | tf_op jit(solution)/shard_map/all_to_all | solution.py:148
  211.0 158.1 %slice-start.1 = ((s8[7340032]{0:T(1024)(128)(4,1)}), s8[4194304]{0:T(1024)(128)(4,1)S(1)}, s32[]{:S(2)}) async-start(s8[7340032]{0:T(1024)(128)(4,1)} %bitcast.68), calls=%async_computation.5 | async-start | bytes 8388608
  398.6 6.8 %copy-start.3 = (bf16[384,14336]{1,0:T(8,128)(2,1)S(1)}, bf16[384,14336]{1,0:T(8,128)(2,1)}, u32[]{:S(2)}) copy-start(bf16[384,14336]{1,0:T(8,128)(2,1)} %select_n.59) | copy-start | bytes 33030148
  405.3 3.8 copy-start.6
  409.2 2.0 copy-start.4
  416.9 126.5 %all-to-all-start.3 = ((bf16[16,24,7168]{2,1,0:T(8,128)(2,1)}), bf16[16,24,7168]{2,1,0:T(8,128)(2,1)}, u32[]{:S(2)}, u32[]{:S(2)}) async-start(bf16[16,24,7168]{2,1,0:T(8,128)(2,1)} %bitcast.70), calls=%async_computation.3 | async-start | bytes 11010048 | tf_op jit(solution)/shard_map/all_to_all | solution.py:152
  423.0 3.6 copy-start.8
  427.3 119.7 %copy-start.10 = (bf16[1,32,7168]{2,1,0:T(8,128)(2,1)S(1)}, bf16[1,32,7168]{2,1,0:T(8,128)(2,1)}, u32[]{:S(2)}) copy-start(bf16[1,32,7168]{2,1,0:T(8,128)(2,1)} %param.14) | copy-start | bytes 1376260
  427.3 121.9 %collective-permute-start.2 = (bf16[1,32,7168]{2,1,0:T(8,128)(2,1)S(1)}, bf16[1,32,7168]{2,1,0:T(8,128)(2,1)S(1)}, u32[]{:S(2)}, u32[]{:S(2)}) collective-permute-start(bf16[1,32,7168]{2,1,0:T(8,128)(2,1)S(1)} %fusion.3), channel_id=1, source_target_pairs={{0,16},{16,0},{1,17},{17,1},{2,18},{18,2},{3,19},{19,3},{4,20},{20... | collective-permute-start | bytes 1376264 | tf_op jit(solution)/shard_map/ppermute | solution.py:23
  547.6 12.8 %collective-permute-start.5 = (bf16[1,32,7168]{2,1,0:T(8,128)(2,1)S(1)}, bf16[1,32,7168]{2,1,0:T(8,128)(2,1)S(1)}, u32[]{:S(2)}, u32[]{:S(2)}) collective-permute-start(bf16[1,32,7168]{2,1,0:T(8,128)(2,1)S(1)} %fusion.2), channel_id=1, source_target_pairs={{0,16},{16,0},{1,17},{17,1},{2,18},{18,2},{3,19},{19,3},{4,20},{20... | collective-permute-start | bytes 1376264 | tf_op jit(solution)/shard_map/ppermute | solution.py:23
where the time goes:
time: 566 us; the launch traced here: 562 us
  waiting for transfers between devices  397 us (70%)
  local copies, waits for them, and re-layouts  74.9 us (13%)
  matrix products  32.7 us (6%)
  starting transfers between devices  30.3 us (5%)
  other arithmetic  26 us (5%)
    ppermute x4, waiting for transfers between devices, from_partner(): return lax.ppermute(block, axis, route)  169 us
    all_to_all x1, waiting for transfers between devices, body(): lax.all_to_all(b_partial, 'ep', split_axis=0, concat_axis=0, tiled=True)  115 us
    all_to_all x1, waiting for transfers between devices, body(): lax.all_to_all(b_slots.reshape(devices, capacity // GROUP, 2 * width), 'e...  68.7 us
    select_n x6, local copies, waits for them, and re-layouts, fill_group(): jnp.where(upper, jnp.concatenate([other, gathered], axis=1), jnp.concaten...  43.7 us
    all_to_all x1, waiting for transfers between devices, body(): lax.all_to_all(f_slots.reshape(devices, capacity // GROUP, width), 'ep',...  33.7 us
    select_n x4, other arithmetic, fill_group(): jnp.where(upper, jnp.concatenate([other, gathered], axis=1), jnp.concaten...  16.6 us
  transfers between devices with their start and end apart: 10, of which 7 were waited for; matrix products, arithmetic and copies ran while one was open for 19% of the time, Pallas kernels for 0%

commit v1 on v0

--- a/solution.py
+++ b/solution.py
@@ -5,6 +5,17 @@
 
 GROUP = 4
 TOPK = 2
+
+
+def in_blocks(value, dim, size):
+    before, after = (value.shape[:dim], value.shape[dim + 1 :])
+    return jnp.moveaxis(value.reshape(*before, size, -1, *after), dim, 0)
+
+
+def laid_out(tiles, dim):
+    tiles = jnp.moveaxis(tiles, 0, dim)
+    dims = tiles.shape
+    return tiles.reshape(*dims[:dim], dims[dim] * dims[dim + 1], *dims[dim + 2 :])
 
 
 def from_partner(block, axis, apart):
@@ -137,13 +148,15 @@
         tiled=True,
     )
     f_partial = forward_rows(fill_group(f_shares, False))
-    b_shares = lax.all_to_all(
-        b_slots.reshape(devices, capacity // GROUP, 2 * width),
-        "ep",
-        split_axis=0,
-        concat_axis=0,
-        tiled=True,
-    )
+    array = b_slots.reshape(devices, capacity // GROUP, 2 * width)
+    size, here = (lax.axis_size("ep"), lax.axis_index("ep"))
+    tiles = in_blocks(array, 0, size)
+    outs = [tiles[here]]
+    for step in range(1, size):
+        sent = tiles[here ^ step]
+        outs.append(lax.ppermute(sent, "ep", [(i, i ^ step) for i in range(size)]))
+    tiles = jnp.stack(outs)[here ^ jnp.arange(size)]
+    b_shares = laid_out(tiles, 0)
     b_partial = backward_rows(fill_group(b_shares, True))
     f_back = lax.all_to_all(f_partial, "ep", split_axis=0, concat_axis=0, tiled=True)
     f_out = jnp.sum(

time: 566 us -> 590 us (1.042)
  local copies, waits for them, and re-layouts: 74.9 us -> 93.4 us
  starting transfers between devices: 30.3 us -> 36.5 us
    ppermute x0 -> x15, waiting for transfers between devices: none -> 98.3 us  [body(): outs.append(lax.ppermute(sent, 'ep', [(i, i ^ step) for i in range(size)]))]
    all_to_all x1 -> x0, waiting for transfers between devices: 68.7 us -> none  [body(): lax.all_to_all(b_slots.reshape(devices, capacity // GROUP, 2 * width), 'e...]
    all_to_all x1, waiting for transfers between devices: 33.7 us -> 0.01 us  [body(): lax.all_to_all(f_slots.reshape(devices, capacity // GROUP, width), 'ep',...]
    ppermute x0 -> x15, starting transfers between devices: none -> 14.7 us  [body(): outs.append(lax.ppermute(sent, 'ep', [(i, i ^ step) for i in range(size)]))]
    unnamed x40 -> x52, local copies, waits for them, and re-layouts: 6.25 us -> 17.3 us
    gather x0 -> x2, local copies, waits for them, and re-layouts: none -> 9.76 us  [body(): tiles = jnp.stack(outs)[here ^ jnp.arange(size)]]
    ppermute x4, waiting for transfers between devices: 169 us -> 177 us  [from_partner(): return lax.ppermute(block, axis, route)]
  transfers between devices with their start and end apart: 10 -> 24, of which waited for: 7 -> 14; matrix products, arithmetic and copies ran while one was open for 19% -> 22% of each run, Pallas kernels for 0% -> 0%
where the time goes in v1:
time: 590 us; the launch traced here: 586 us
  waiting for transfers between devices  401 us (68%)
  local copies, waits for them, and re-layouts  93.4 us (16%)
  starting transfers between devices  36.5 us (6%)
  matrix products  31.4 us (5%)
  other arithmetic  22.3 us (4%)
    ppermute x4, waiting for transfers between devices, from_partner(): return lax.ppermute(block, axis, route)  177 us
    all_to_all x1, waiting for transfers between devices, body(): lax.all_to_all(b_partial, 'ep', split_axis=0, concat_axis=0, tiled=True)  114 us
    ppermute x15, waiting for transfers between devices, body(): outs.append(lax.ppermute(sent, 'ep', [(i, i ^ step) for i in range(size)]))  98.3 us
    select_n x6, local copies, waits for them, and re-layouts, fill_group(): jnp.where(upper, jnp.concatenate([other, gathered], axis=1), jnp.concaten...  43.6 us
    unnamed x52, local copies, waits for them, and re-layouts  17.3 us
    ppermute x15, starting transfers between devices, body(): outs.append(lax.ppermute(sent, 'ep', [(i, i ^ step) for i in range(size)]))  14.7 us
    select_n x4, other arithmetic, fill_group(): jnp.where(upper, jnp.concatenate([other, gathered], axis=1), jnp.concaten...  12.9 us
  transfers between devices with their start and end apart: 24, of which 14 were waited for; matrix products, arithmetic and copies ran while one was open for 22% of the time, Pallas kernels for 0%

profile of v1, /device:TPU:10, one launch (start us, length us, event | category | flops | bytes accessed | tf_op | source)
XLA Modules:
  0.0 585.9 jit_solution(2897774202438997750)
XLA Ops:
  3.6 2.0 convolution_convert_fusion
  5.6 2.7 reshape_reshape_reshape.3
  8.4 3.8 dynamic-slice_bitcast_fusion
  18.8 6.7 %all-to-all-start = ((bf16[16,6,7168]{2,1,0:T(8,128)(2,1)}), bf16[16,6,7168]{2,1,0:T(8,128)(2,1)S(1)}, u32[]{:S(2)}, u32[]{:S(2)}) async-start(bf16[16,6,7168]{2,1,0:T(8,128)(2,1)} %reshape_reshape.2), calls=%async_computation | async-start | bytes 3670016 | tf_op jit(solution)/shard_map/all_to_all | solution.py:143
  26.3 2.4 collective-permute-start.9
  29.4 2.4 collective-permute-start.10
  33.7 2.4 collective-permute-start.12
  36.8 25.9 %collective-permute-done.8 = bf16[1,6,14336]{2,1,0:T(8,128)(2,1)S(1)} collective-permute-done((bf16[1,6,14336]{2,1,0:T(8,128)(2,1)}, bf16[1,6,14336]{2,1,0:T(8,128)(2,1)S(1)}, u32[]{:S(2)}, u32[]{:S(2)}) %collective-permute-start.8) | collective-permute-done | bytes 172064 | tf_op jit(solution)/shard_map/ppermute | solution.py:157
  62.7 1.8 collective-permute-start.13
  65.1 4.5 collective-permute-done.9
  71.6 25.0 %collective-permute-done.10 = bf16[1,6,14336]{2,1,0:T(8,128)(2,1)S(1)} collective-permute-done((bf16[1,6,14336]{2,1,0:T(8,128)(2,1)}, bf16[1,6,14336]{2,1,0:T(8,128)(2,1)S(1)}, u32[]{:S(2)}, u32[]{:S(2)}) %collective-permute-start.10) | collective-permute-done | bytes 172064 | tf_op jit(solution)/shard_map/ppermute | solution.py:157
  97.6 11.1 %collective-permute-done.11 = bf16[1,6,14336]{2,1,0:T(8,128)(2,1)S(1)} collective-permute-done((bf16[1,6,14336]{2,1,0:T(8,128)(2,1)}, bf16[1,6,14336]{2,1,0:T(8,128)(2,1)S(1)}, u32[]{:S(2)}, u32[]{:S(2)}) %collective-permute-start.11) | collective-permute-done | bytes 172064 | tf_op jit(solution)/shard_map/ppermute | solution.py:157
  109.5 6.7 %collective-permute-done.12 = bf16[1,6,14336]{2,1,0:T(8,128)(2,1)S(1)} collective-permute-done((bf16[1,6,14336]{2,1,0:T(8,128)(2,1)S(1)}, bf16[1,6,14336]{2,1,0:T(8,128)(2,1)S(1)}, u32[]{:S(2)}, u32[]{:S(2)}) %collective-permute-start.12) | collective-permute-done | bytes 172064 | tf_op jit(solution)/shard_map/ppermute | solution.py:157
  116.9 4.3 collective-permute-done.13
  121.9 11.0 %collective-permute-done.14 = bf16[1,6,14336]{2,1,0:T(8,128)(2,1)S(1)} collective-permute-done((bf16[1,6,14336]{2,1,0:T(8,128)(2,1)}, bf16[1,6,14336]{2,1,0:T(8,128)(2,1)S(1)}, u32[]{:S(2)}, u32[]{:S(2)}) %collective-permute-start.14) | collective-permute-done | bytes 172064 | tf_op jit(solution)/shard_map/ppermute | solution.py:157
  133.6 3.2 collective-permute-done.15
  137.6 5.2 collective-permute-done.16
  143.4 1.9 copy.54
  147.4 4.7 gather_fusion
  152.1 5.1 copy.63
  159.2 1.9 copy-done.2
  161.2 3.2 copy.57
  165.8 3.5 copy.64
  169.2 2.5 maximum_select_fusion.2
  171.7 5.4 copy.66
  177.7 49.4 %collective-permute-done.1 = bf16[16,2,6,7168]{3,0,2,1:T(8,128)(2,1)S(1)} collective-permute-done((bf16[16,2,6,7168]{3,0,2,1:T(8,128)(2,1)}, bf16[16,2,6,7168]{3,0,2,1:T(8,128)(2,1)S(1)}, u32[]{:S(2)}, u32[]{:S(2)}) %collective-permute-start.1) | collective-permute-done | bytes 2752544 | tf_op jit(solution)/shard_map/ppermute | solution.py:28
  228.6 3.2 maximum_select_fusion.1
  231.8 3.7 copy.60
  235.4 8.5 %select_n.112 = bf16[384,7168]{1,0:T(8,128)(2,1)} reshape(bf16[16,4,6,7168]{3,2,1,0:T(8,128)(2,1)} %copy.60) | data formatting | bytes 11010048 | tf_op jit(solution)/shard_map/jit(_where)/select_n | solution.py:107
  244.0 5.4 fusion.19
  252.3 4.0 convolution_convert_fusion.1
  256.3 4.9 all-to-all-start.1
  261.2 128.1 %collective-permute-done.19 = bf16[16,2,6,14336]{3,0,2,1:T(8,128)(2,1)} collective-permute-done((bf16[16,2,6,14336]{3,0,2,1:T(8,128)(2,1)}, bf16[16,2,6,14336]{3,0,2,1:T(8,128)(2,1)}, u32[]{:S(2)}, u32[]{:S(2)}) %collective-permute-start.19) | collective-permute-done | bytes 5505056 | tf_op jit(solution)/shard_map/ppermute | solution.py:28
  389.3 5.6 copy.67
  395.0 6.3 %maximum_select_fusion = bf16[16,4,6,14336]{3,2,0,1:T(8,128)(2,1)S(1)} fusion(bf16[16,2,6,14336]{3,2,0,1:T(8,128)(2,1)S(1)} %bitcast.132, bf16[16,2,6,14336]{3,2,0,1:T(8,128)(2,1)S(1)} %copy.67, pred[]{:T(512)S(6)} %eq.71), kind=kLoop, calls=%fused_computation.2 | loop fusion | flops 16515072 | bytes 22020096 | tf_op jit(solution)/shard_map/jit(_where)/select_n | solution.py:107
  401.3 6.4 %copy.69 = bf16[16,4,6,14336]{3,2,1,0:T(8,128)(2,1)} copy(bf16[16,4,6,14336]{3,2,0,1:T(8,128)(2,1)S(1)} %maximum_select_fusion) | data formatting | bytes 22020096 | tf_op jit(solution)/shard_map/jit(_where)/select_n | solution.py:107
  407.7 16.5 %select_n.134 = bf16[384,14336]{1,0:T(8,128)(2,1)} reshape(bf16[16,4,6,14336]{3,2,1,0:T(8,128)(2,1)} %copy.69) | data formatting | bytes 22020096 | tf_op jit(solution)/shard_map/jit(_where)/select_n | solution.py:107
  424.1 5.4 fusion.4
  430.9 3.8 fusion.6
  434.8 1.6 fusion.39
  436.8 1.6 fusion.16
  438.4 4.1 add_convert_fusion
  442.5 4.7 all-to-all-start.2
  447.2 3.6 bitcast_reduce_fusion.1
  453.1 114.0 %all-to-all-done.2 = bf16[16,24,7168]{2,1,0:T(8,128)(2,1)} async-done(((bf16[16,24,7168]{2,1,0:T(8,128)(2,1)}), bf16[16,24,7168]{2,1,0:T(8,128)(2,1)}, u32[]{:S(2)}, u32[]{:S(2)}) %all-to-all-start.2) | async-done | bytes 5505056 | tf_op jit(solution)/shard_map/all_to_all | solution.py:165
  567.1 3.5 bitcast_reduce_fusion
  571.4 1.6 collective-permute-start.20
  572.9 11.2 %collective-permute-done.20 = bf16[1,32,7168]{2,1,0:T(8,128)(2,1)S(1)} collective-permute-done((bf16[1,32,7168]{2,1,0:T(8,128)(2,1)S(1)}, bf16[1,32,7168]{2,1,0:T(8,128)(2,1)S(1)}, u32[]{:S(2)}, u32[]{:S(2)}) %collective-permute-start.20) | collective-permute-done | bytes 458784 | tf_op jit(solution)/shard_map/ppermute | solution.py:34
  (106 shorter events, 38.3 us)
Async XLA Ops:
  8.4 7.5 %copy-start.13 = (s32[1,32,2]{1,2,0:T(2,128)S(1)}, s32[1,32,2]{1,2,0:T(2,128)}, u32[]{:S(2)}) copy-start(s32[1,32,2]{1,2,0:T(2,128)} %param.11) | copy-start | bytes 772
  8.4 8.2 %copy-start.14 = (f32[1,32,2]{1,2,0:T(2,128)S(1)}, f32[1,32,2]{1,2,0:T(2,128)}, u32[]{:S(2)}) copy-start(f32[1,32,2]{1,2,0:T(2,128)} %param.12) | copy-start | bytes 772
  8.4 8.3 %copy-start.10 = (bf16[1,32,7168]{2,1,0:T(8,128)(2,1)S(1)}, bf16[1,32,7168]{2,1,0:T(8,128)(2,1)}, u32[]{:S(2)}) copy-start(bf16[1,32,7168]{2,1,0:T(8,128)(2,1)} %param.10) | copy-start | bytes 1376260
  12.2 13.3 %collective-permute-start.3 = (bf16[1,6,14336]{2,1,0:T(8,128)(2,1)}, bf16[1,6,14336]{2,1,0:T(8,128)(2,1)S(1)}, u32[]{:S(2)}, u32[]{:S(2)}) collective-permute-start(bf16[1,6,14336]{2,1,0:T(8,128)(2,1)} %get-tuple-element.20), channel_id=1, source_target_pairs={{0,1},{1,0},{2,3},{3,2},{4,5},{5,4},{6,7},{7,6},{8,9},{9,8},{10,11... | collective-permute-start | bytes 516104 | tf_op jit(solution)/shard_map/ppermute | solution.py:157
  12.3 14.0 %collective-permute-start.4 = (bf16[1,6,14336]{2,1,0:T(8,128)(2,1)}, bf16[1,6,14336]{2,1,0:T(8,128)(2,1)S(1)}, u32[]{:S(2)}, u32[]{:S(2)}) collective-permute-start(bf16[1,6,14336]{2,1,0:T(8,128)(2,1)} %get-tuple-element.19), channel_id=1, source_target_pairs={{0,2},{1,3},{2,0},{3,1},{4,6},{5,7},{6,4},{7,5},{8,10},{9,11},{10,... | collective-permute-start | bytes 516104 | tf_op jit(solution)/shard_map/ppermute | solution.py:157
  12.9 16.5 %collective-permute-start.5 = (bf16[1,6,14336]{2,1,0:T(8,128)(2,1)}, bf16[1,6,14336]{2,1,0:T(8,128)(2,1)S(1)}, u32[]{:S(2)}, u32[]{:S(2)}) collective-permute-start(bf16[1,6,14336]{2,1,0:T(8,128)(2,1)} %get-tuple-element.18), channel_id=1, source_target_pairs={{0,3},{1,2},{2,1},{3,0},{4,7},{5,6},{6,5},{7,4},{8,11},{9,10},{10,... | collective-permute-start | bytes 516104 | tf_op jit(solution)/shard_map/ppermute | solution.py:157
  14.2 18.3 %collective-permute-start.6 = (bf16[1,6,14336]{2,1,0:T(8,128)(2,1)}, bf16[1,6,14336]{2,1,0:T(8,128)(2,1)S(1)}, u32[]{:S(2)}, u32[]{:S(2)}) collective-permute-start(bf16[1,6,14336]{2,1,0:T(8,128)(2,1)} %get-tuple-element.17), channel_id=1, source_target_pairs={{0,4},{1,5},{2,6},{3,7},{4,0},{5,1},{6,2},{7,3},{8,12},{9,13},{10,... | collective-permute-start | bytes 516104 | tf_op jit(solution)/shard_map/ppermute | solution.py:157
  14.6 19.1 %collective-permute-start.7 = (bf16[1,6,14336]{2,1,0:T(8,128)(2,1)}, bf16[1,6,14336]{2,1,0:T(8,128)(2,1)S(1)}, u32[]{:S(2)}, u32[]{:S(2)}) collective-permute-start(bf16[1,6,14336]{2,1,0:T(8,128)(2,1)} %get-tuple-element.16), channel_id=1, source_target_pairs={{0,5},{1,4},{2,7},{3,6},{4,1},{5,0},{6,3},{7,2},{8,13},{9,12},{10,... | collective-permute-start | bytes 516104 | tf_op jit(solution)/shard_map/ppermute | solution.py:157
  18.8 124.6 %all-to-all-start = ((bf16[16,6,7168]{2,1,0:T(8,128)(2,1)}), bf16[16,6,7168]{2,1,0:T(8,128)(2,1)S(1)}, u32[]{:S(2)}, u32[]{:S(2)}) async-start(bf16[16,6,7168]{2,1,0:T(8,128)(2,1)} %reshape_reshape.2), calls=%async_computation | async-start | bytes 3670016 | tf_op jit(solution)/shard_map/all_to_all | solution.py:143
  25.5 37.1 %collective-permute-start.8 = (bf16[1,6,14336]{2,1,0:T(8,128)(2,1)}, bf16[1,6,14336]{2,1,0:T(8,128)(2,1)S(1)}, u32[]{:S(2)}, u32[]{:S(2)}) collective-permute-start(bf16[1,6,14336]{2,1,0:T(8,128)(2,1)} %get-tuple-element.15), channel_id=1, source_target_pairs={{0,6},{1,7},{2,4},{3,5},{4,2},{5,3},{6,0},{7,1},{8,14},{9,15},{10,... | collective-permute-start | bytes 516104 | tf_op jit(solution)/shard_map/ppermute | solution.py:157
  26.3 43.4 %collective-permute-start.9 = (bf16[1,6,14336]{2,1,0:T(8,128)(2,1)}, bf16[1,6,14336]{2,1,0:T(8,128)(2,1)S(1)}, u32[]{:S(2)}, u32[]{:S(2)}) collective-permute-start(bf16[1,6,14336]{2,1,0:T(8,128)(2,1)} %get-tuple-element.14), channel_id=1, source_target_pairs={{0,7},{1,6},{2,5},{3,4},{4,3},{5,2},{6,1},{7,0},{8,15},{9,14},{10,... | collective-permute-start | bytes 516104 | tf_op jit(solution)/shard_map/ppermute | solution.py:157
  29.4 67.2 %collective-permute-start.10 = (bf16[1,6,14336]{2,1,0:T(8,128)(2,1)}, bf16[1,6,14336]{2,1,0:T(8,128)(2,1)S(1)}, u32[]{:S(2)}, u32[]{:S(2)}) collective-permute-start(bf16[1,6,14336]{2,1,0:T(8,128)(2,1)} %get-tuple-element.13), channel_id=1, source_target_pairs={{0,8},{1,9},{2,10},{3,11},{4,12},{5,13},{6,14},{7,15},{8,0},{9,1},... | collective-permute-start | bytes 516104 | tf_op jit(solution)/shard_map/ppermute | solution.py:157
  32.5 76.3 %collective-permute-start.11 = (bf16[1,6,14336]{2,1,0:T(8,128)(2,1)}, bf16[1,6,14336]{2,1,0:T(8,128)(2,1)S(1)}, u32[]{:S(2)}, u32[]{:S(2)}) collective-permute-start(bf16[1,6,14336]{2,1,0:T(8,128)(2,1)} %get-tuple-element.12), channel_id=1, source_target_pairs={{0,9},{1,8},{2,11},{3,10},{4,13},{5,12},{6,15},{7,14},{8,1},{9,0},... | collective-permute-start | bytes 516104 | tf_op jit(solution)/shard_map/ppermute | solution.py:157
  33.7 82.5 %collective-permute-start.12 = (bf16[1,6,14336]{2,1,0:T(8,128)(2,1)S(1)}, bf16[1,6,14336]{2,1,0:T(8,128)(2,1)S(1)}, u32[]{:S(2)}, u32[]{:S(2)}) collective-permute-start(bf16[1,6,14336]{2,1,0:T(8,128)(2,1)S(1)} %get-tuple-element.11), channel_id=1, source_target_pairs={{0,10},{1,11},{2,8},{3,9},{4,14},{5,15},{6,12},{7,13},{8,2},{9,3},... | collective-permute-start | bytes 516104 | tf_op jit(solution)/shard_map/ppermute | solution.py:157
  62.7 58.5 %collective-permute-start.13 = (bf16[1,6,14336]{2,1,0:T(8,128)(2,1)}, bf16[1,6,14336]{2,1,0:T(8,128)(2,1)S(1)}, u32[]{:S(2)}, u32[]{:S(2)}) collective-permute-start(bf16[1,6,14336]{2,1,0:T(8,128)(2,1)} %get-tuple-element.10), channel_id=1, source_target_pairs={{0,11},{1,10},{2,9},{3,8},{4,15},{5,14},{6,13},{7,12},{8,3},{9,2},... | collective-permute-start | bytes 516104 | tf_op jit(solution)/shard_map/ppermute | solution.py:157
  69.7 63.2 %collective-permute-start.14 = (bf16[1,6,14336]{2,1,0:T(8,128)(2,1)}, bf16[1,6,14336]{2,1,0:T(8,128)(2,1)S(1)}, u32[]{:S(2)}, u32[]{:S(2)}) collective-permute-start(bf16[1,6,14336]{2,1,0:T(8,128)(2,1)} %get-tuple-element.9), channel_id=1, source_target_pairs={{0,12},{1,13},{2,14},{3,15},{4,8},{5,9},{6,10},{7,11},{8,4},{9,5},... | collective-permute-start | bytes 516104 | tf_op jit(solution)/shard_map/ppermute | solution.py:157
  96.6 40.3 %collective-permute-start.15 = (bf16[1,6,14336]{2,1,0:T(8,128)(2,1)}, bf16[1,6,14336]{2,1,0:T(8,128)(2,1)S(1)}, u32[]{:S(2)}, u32[]{:S(2)}) collective-permute-start(bf16[1,6,14336]{2,1,0:T(8,128)(2,1)} %get-tuple-element.8), channel_id=1, source_target_pairs={{0,13},{1,12},{2,15},{3,14},{4,9},{5,8},{6,11},{7,10},{8,5},{9,4},... | collective-permute-start | bytes 516104 | tf_op jit(solution)/shard_map/ppermute | solution.py:157
  108.8 34.0 %collective-permute-start.16 = (bf16[1,6,14336]{2,1,0:T(8,128)(2,1)S(1)}, bf16[1,6,14336]{2,1,0:T(8,128)(2,1)S(1)}, u32[]{:S(2)}, u32[]{:S(2)}) collective-permute-start(bf16[1,6,14336]{2,1,0:T(8,128)(2,1)S(1)} %get-tuple-element.7), channel_id=1, source_target_pairs={{0,14},{1,15},{2,12},{3,13},{4,10},{5,11},{6,8},{7,9},{8,6},{9,7},... | collective-permute-start | bytes 516104 | tf_op jit(solution)/shard_map/ppermute | solution.py:157
  116.2 30.5 %collective-permute-start.17 = (bf16[1,6,14336]{2,1,0:T(8,128)(2,1)}, bf16[1,6,14336]{2,1,0:T(8,128)(2,1)S(1)}, u32[]{:S(2)}, u32[]{:S(2)}) collective-permute-start(bf16[1,6,14336]{2,1,0:T(8,128)(2,1)} %get-tuple-element.6), channel_id=1, source_target_pairs={{0,15},{1,14},{2,13},{3,12},{4,11},{5,10},{6,9},{7,8},{8,7},{9,6},... | collective-permute-start | bytes 516104 | tf_op jit(solution)/shard_map/ppermute | solution.py:157
  145.4 12.1 %collective-permute-start = (bf16[16,1,6,7168]{3,0,2,1:T(8,128)(2,1)}, bf16[16,1,6,7168]{3,0,2,1:T(8,128)(2,1)S(1)}, u32[]{:S(2)}, u32[]{:S(2)}) collective-permute-start(bf16[16,1,6,7168]{3,0,2,1:T(8,128)(2,1)} %copy.54), channel_id=1, source_target_pairs={{0,1},{1,0},{2,3},{3,2},{4,5},{5,4},{6,7},{7,6},{8,9},{9,8},{10,11... | collective-permute-start | bytes 4128776 | tf_op jit(solution)/shard_map/ppermute | solution.py:28
  157.2 8.6 %collective-permute-start.18 = (bf16[16,1,6,14336]{3,0,2,1:T(8,128)(2,1)}, bf16[16,1,6,14336]{3,0,2,1:T(8,128)(2,1)}, u32[]{:S(2)}, u32[]{:S(2)}) collective-permute-start(bf16[16,1,6,14336]{3,0,2,1:T(8,128)(2,1)} %copy.63), channel_id=1, source_target_pairs={{0,1},{1,0},{2,3},{3,2},{4,5},{5,4},{6,7},{7,6},{8,9},{9,8},{10,11... | collective-permute-start | bytes 8257544 | tf_op jit(solution)/shard_map/ppermute | solution.py:28
  159.2 1.9 copy-start.2
  164.3 62.7 %collective-permute-start.1 = (bf16[16,2,6,7168]{3,0,2,1:T(8,128)(2,1)}, bf16[16,2,6,7168]{3,0,2,1:T(8,128)(2,1)S(1)}, u32[]{:S(2)}, u32[]{:S(2)}) collective-permute-start(bf16[16,2,6,7168]{3,0,2,1:T(8,128)(2,1)} %copy.57), channel_id=1, source_target_pairs={{0,2},{2,0},{1,3},{3,1},{4,6},{6,4},{5,7},{7,5},{8,10},{10,8},{9,1... | collective-permute-start | bytes 8257544 | tf_op jit(solution)/shard_map/ppermute | solution.py:28
  165.8 3.5 copy-start.1
  171.7 5.4 copy-start
  177.1 51.5 %copy-start.3 = (bf16[16,2,6,7168]{3,2,0,1:T(8,128)(2,1)S(1)}, bf16[16,2,6,7168]{3,2,0,1:T(8,128)(2,1)}, u32[]{:S(2)}) copy-start(bf16[16,2,6,7168]{3,2,0,1:T(8,128)(2,1)} %copy-done.2) | copy-start | bytes 8257540
  177.1 212.3 %collective-permute-start.19 = (bf16[16,2,6,14336]{3,0,2,1:T(8,128)(2,1)}, bf16[16,2,6,14336]{3,0,2,1:T(8,128)(2,1)}, u32[]{:S(2)}, u32[]{:S(2)}) collective-permute-start(bf16[16,2,6,14336]{3,0,2,1:T(8,128)(2,1)} %copy.66), channel_id=1, source_target_pairs={{0,2},{2,0},{1,3},{3,1},{4,6},{6,4},{5,7},{7,5},{8,10},{10,8},{9,1... | collective-permute-start | bytes 16515080 | tf_op jit(solution)/shard_map/ppermute | solution.py:28
  244.0 5.4 copy-start.5
  244.0 6.3 %copy-start.7 = (bf16[1,7168,256]{2,1,0:T(8,128)(2,1)S(1)}, bf16[1,7168,256]{2,1,0:T(8,128)(2,1)}, u32[]{:S(2)}) copy-start(bf16[1,7168,256]{2,1,0:T(8,128)(2,1)} %param.18) | copy-start | bytes 11010052
  250.3 2.0 copy-start.9
  256.3 138.7 %slice-start = ((s8[7340032]{0:T(1024)(128)(4,1)}), s8[3145728]{0:T(1024)(128)(4,1)S(1)}, s32[]{:S(2)}) async-start(s8[7340032]{0:T(1024)(128)(4,1)} %bitcast.131), calls=%async_computation.3 | async-start | bytes 6291456
  256.3 186.2 %all-to-all-start.1 = ((bf16[16,24,7168]{2,1,0:T(8,128)(2,1)}), bf16[16,24,7168]{2,1,0:T(8,128)(2,1)}, u32[]{:S(2)}, u32[]{:S(2)}) async-start(bf16[16,24,7168]{2,1,0:T(8,128)(2,1)} %bitcast.136), calls=%async_computation.1 | async-start | bytes 11010048 | tf_op jit(solution)/shard_map/all_to_all | solution.py:161
  261.2 133.8 %slice-start.1 = ((s8[7340032]{0:T(1024)(128)(4,1)}), s8[4194304]{0:T(1024)(128)(4,1)S(1)}, s32[]{:S(2)}) async-start(s8[7340032]{0:T(1024)(128)(4,1)} %bitcast.131), calls=%async_computation.4 | async-start | bytes 8388608
  424.1 6.8 %copy-start.4 = (bf16[384,14336]{1,0:T(8,128)(2,1)S(1)}, bf16[384,14336]{1,0:T(8,128)(2,1)}, u32[]{:S(2)}) copy-start(bf16[384,14336]{1,0:T(8,128)(2,1)} %select_n.134) | copy-start | bytes 33030148
  430.9 3.8 copy-start.8
  434.8 2.0 copy-start.6
  442.5 124.6 %all-to-all-start.2 = ((bf16[16,24,7168]{2,1,0:T(8,128)(2,1)}), bf16[16,24,7168]{2,1,0:T(8,128)(2,1)}, u32[]{:S(2)}, u32[]{:S(2)}) async-start(bf16[16,24,7168]{2,1,0:T(8,128)(2,1)} %bitcast.135), calls=%async_computation.2 | async-start | bytes 11010048 | tf_op jit(solution)/shard_map/all_to_all | solution.py:165
  447.2 3.6 copy-start.11
  451.5 119.1 %copy-start.12 = (bf16[1,32,7168]{2,1,0:T(8,128)(2,1)S(1)}, bf16[1,32,7168]{2,1,0:T(8,128)(2,1)}, u32[]{:S(2)}) copy-start(bf16[1,32,7168]{2,1,0:T(8,128)(2,1)} %param.14) | copy-start | bytes 1376260
  451.5 121.4 %collective-permute-start.2 = (bf16[1,32,7168]{2,1,0:T(8,128)(2,1)S(1)}, bf16[1,32,7168]{2,1,0:T(8,128)(2,1)S(1)}, u32[]{:S(2)}, u32[]{:S(2)}) collective-permute-start(bf16[1,32,7168]{2,1,0:T(8,128)(2,1)S(1)} %fusion.3), channel_id=1, source_target_pairs={{0,16},{16,0},{1,17},{17,1},{2,18},{18,2},{3,19},{19,3},{4,20},{20... | collective-permute-start | bytes 1376264 | tf_op jit(solution)/shard_map/ppermute | solution.py:34
  571.4 12.8 %collective-permute-start.20 = (bf16[1,32,7168]{2,1,0:T(8,128)(2,1)S(1)}, bf16[1,32,7168]{2,1,0:T(8,128)(2,1)S(1)}, u32[]{:S(2)}, u32[]{:S(2)}) collective-permute-start(bf16[1,32,7168]{2,1,0:T(8,128)(2,1)S(1)} %fusion.2), channel_id=1, source_target_pairs={{0,16},{16,0},{1,17},{17,1},{2,18},{18,2},{3,19},{19,3},{4,20},{20... | collective-permute-start | bytes 1376264 | tf_op jit(solution)/shard_map/ppermute | solution.py:34
